TPU v7x, 512 devices: a whole 4x8x8 slice. The times are simulated.
512 devices in a mesh: ctx: 64 (over y_hi, x, z), head: 8 (over y_lo, core).
Axes of the slice: x: 4, y: 8 (y_hi: 2, y_lo: 4; y = y_hi * 4 + y_lo), z: 8, core: 2. Of those that a mesh axis runs over, the one named last changes fastest.
Arguments:
- q_self: bfloat16 [8192, 4096], P('ctx', 'head'), may hold values from -6 to 6
- k_self: bfloat16 [8192, 4096], P('ctx', 'head'), may hold values from -6 to 6
- v_self: bfloat16 [8192, 4096], P('ctx', 'head'), may hold values from -6 to 6
- q_cross: bfloat16 [8192, 4096], P('ctx', 'head'), may hold values from -6 to 6
- n_keys: bfloat16 [32768, 4096], P('ctx', 'head'), may hold values from -6 to 6
- n_values: bfloat16 [32768, 4096], P('ctx', 'head'), may hold values from -6 to 6
- d_cross: bfloat16 [8192, 4096], P('ctx', 'head'), may hold values from -16 to 16
Outputs:
- self_out: bfloat16 [8192, 4096], P('ctx', 'head')
- cross_out: bfloat16 [8192, 4096], P('ctx', 'head')
- d_query: bfloat16 [8192, 4096], P('ctx', 'head')
- d_keys: bfloat16 [32768, 4096], P('ctx', 'head')
- d_values: bfloat16 [32768, 4096], P('ctx', 'head')
All inputs are finite; a program needn't handle non-finite values.
Results may differ from a plain program's by a relative error of at most 0.012.
Values may be sent and summed in bfloat16 or wider, within the bound.
No kernel may reach another device: no remote copies, remote signals or barrier semaphores. Data moves between devices by JAX's collectives and lax.ppermute only.
A program may use at most 128 MiB of HBM per device.

v0:
```python
import math
import jax
import jax.numpy as jnp
from jax import lax
from jax.sharding import PartitionSpec as P

HD = 128
SPAN = 64


def from_behind(block, axis, distance):
    devices = range(lax.axis_size(axis))
    route = [(i - distance, i) for i in devices if i - distance in devices]
    return lax.ppermute(block, axis, route)


def attend_block(folded, keys_block, values_block, key_first, queries, positions):
    running_max, running_sum, accumulated = folded
    scores = jnp.einsum("rhd,khd->hrk", queries, keys_block, preferred_element_type=jnp.float32) * (
        1.0 / math.sqrt(HD)
    )
    key_positions = key_first + jnp.arange(keys_block.shape[0], dtype=jnp.int32)
    visible = (key_positions[None, :] <= positions[:, None])[None]
    masked = jnp.where(visible, scores, jnp.float32(-1e30))
    new_max = jnp.maximum(running_max, jnp.max(masked, axis=2))
    weights = jnp.where(visible, jnp.exp(masked - new_max[:, :, None]), jnp.float32(0.0))
    rescale = jnp.exp(running_max - new_max)
    new_sum = running_sum * rescale + jnp.sum(weights, axis=2)
    product = jnp.einsum(
        "hrk,khd->hrd",
        weights.astype(jnp.bfloat16),
        values_block,
        preferred_element_type=jnp.float32,
    )
    return (new_max, new_sum, accumulated * rescale[:, :, None] + product)


def self_attention(groups, keys_local, values_local):
    column_count = keys_local.shape[1]
    head_count = column_count // HD
    prepared = []
    for queries_flat, positions in groups:
        row_count = queries_flat.shape[0]
        prepared.append(
            (queries_flat.reshape(row_count, head_count, HD), positions, jnp.max(positions))
        )
    initial = tuple(
        (
            (
                jnp.full((head_count, entry[0].shape[0]), -1e30, jnp.float32),
                jnp.zeros((head_count, entry[0].shape[0]), jnp.float32),
                jnp.zeros((head_count, entry[0].shape[0], HD), jnp.float32),
            )
            for entry in prepared
        )
    )
    folded = initial
    keys_piece = lax.all_gather(keys_local, "ctx", axis=0, tiled=True)
    values_piece = lax.all_gather(values_local, "ctx", axis=0, tiled=True)
    piece_rows = keys_piece.shape[0]
    block_rows = 512
    block_count = piece_rows // block_rows
    key_blocks = keys_piece.reshape(block_count, block_rows, head_count, HD)
    value_blocks = values_piece.reshape(block_count, block_rows, head_count, HD)

    def visit(inner, items):
        keys_block, values_block, block_index = items
        key_first = block_index * block_rows
        updated = []
        for state, entry in zip(inner, prepared):
            queries, positions, last_position = entry

            def update(current, queries=queries, positions=positions):
                return attend_block(
                    current, keys_block, values_block, key_first, queries, positions
                )

            def unchanged(current):
                return current

            updated.append(lax.cond(key_first <= last_position, update, unchanged, state))
        return (tuple(updated), None)

    folded, unused = lax.scan(
        visit, folded, (key_blocks, value_blocks, jnp.arange(block_count, dtype=jnp.int32))
    )
    outputs = []
    for state in folded:
        running_max, running_sum, accumulated = state
        mixed = accumulated / running_sum[:, :, None]
        row_count = mixed.shape[1]
        outputs.append(
            mixed.transpose(1, 0, 2).reshape(row_count, column_count).astype(jnp.bfloat16)
        )
    return outputs


def cross_attention(q_cross, n_keys, n_values, d_cross):
    row_count, column_count = q_cross.shape
    head_count = column_count // HD
    lag_rows = SPAN - 1
    scale_factor = 1.0 / math.sqrt(HD)
    incoming = from_behind(q_cross[:lag_rows], "ctx", -1)
    shifted = jnp.concatenate([q_cross[lag_rows:], incoming], axis=0)
    span_count = row_count // SPAN
    neighbour_rows = n_keys.shape[0] // span_count
    queries = shifted.reshape(span_count, SPAN, head_count, HD)
    neighbour_keys = n_keys.reshape(span_count, neighbour_rows, head_count, HD)
    neighbour_values = n_values.reshape(span_count, neighbour_rows, head_count, HD)
    grad_rows = d_cross.reshape(span_count, SPAN, head_count, HD)
    scores = (
        jnp.einsum("crhd,ckhd->chrk", queries, neighbour_keys, preferred_element_type=jnp.float32)
        * scale_factor
    )
    row_max = jnp.max(scores, axis=3, keepdims=True)
    weights = jnp.exp(scores - row_max)
    probs = weights / jnp.sum(weights, axis=3, keepdims=True)
    probs_low = probs.astype(jnp.bfloat16)
    attended = jnp.einsum(
        "chrk,ckhd->crhd", probs_low, neighbour_values, preferred_element_type=jnp.float32
    )
    cross_out = attended.reshape(row_count, column_count).astype(jnp.bfloat16)
    grad_probs = jnp.einsum(
        "crhd,ckhd->chrk", grad_rows, neighbour_values, preferred_element_type=jnp.float32
    )
    centre = jnp.sum(grad_probs * probs, axis=3, keepdims=True)
    grad_scores = (probs * (grad_probs - centre) * scale_factor).astype(jnp.bfloat16)
    grad_source = jnp.einsum(
        "chrk,ckhd->crhd", grad_scores, neighbour_keys, preferred_element_type=jnp.float32
    )
    grad_source = grad_source.reshape(row_count, column_count).astype(jnp.bfloat16)
    grad_keys = jnp.einsum(
        "chrk,crhd->ckhd", grad_scores, queries, preferred_element_type=jnp.float32
    ).reshape(n_keys.shape)
    grad_values = jnp.einsum(
        "chrk,crhd->ckhd", probs_low, grad_rows, preferred_element_type=jnp.float32
    ).reshape(n_values.shape)
    carried = from_behind(grad_source[row_count - lag_rows :], "ctx", 1)
    d_query = jnp.concatenate([carried, grad_source[: row_count - lag_rows]], axis=0)
    squares = jnp.sum(grad_keys * grad_keys) + jnp.sum(grad_values * grad_values)
    overall = lax.psum(squares, ("ctx", "head"))
    element_count = 2.0 * grad_keys.size * lax.axis_size("ctx") * lax.axis_size("head")
    factor = lax.rsqrt(overall / element_count + 1e-06)
    d_keys = (grad_keys * factor).astype(jnp.bfloat16)
    d_values = (grad_values * factor).astype(jnp.bfloat16)
    return (cross_out, d_query, d_keys, d_values)


def body(q_self, k_self, v_self, q_cross, n_keys, n_values, d_cross):
    row_count = q_self.shape[0]
    device_index = lax.axis_index("ctx")
    first_row = device_index * row_count
    own_positions = first_row + jnp.arange(row_count, dtype=jnp.int32)
    self_out = self_attention([(q_self, own_positions)], k_self, v_self)[0]
    cross_out, d_query, d_keys, d_values = cross_attention(q_cross, n_keys, n_values, d_cross)
    return (self_out, cross_out, d_query, d_keys, d_values)


def solution(mesh):
    in_specs = (
        P("ctx", "head"),
        P("ctx", "head"),
        P("ctx", "head"),
        P("ctx", "head"),
        P("ctx", "head"),
        P("ctx", "head"),
        P("ctx", "head"),
    )
    out_specs = (
        P("ctx", "head"),
        P("ctx", "head"),
        P("ctx", "head"),
        P("ctx", "head"),
        P("ctx", "head"),
    )
    return jax.shard_map(body, mesh=mesh, in_specs=in_specs, out_specs=out_specs, check_vma=False)
```

profile of v0, /device:TPU:54, one launch (start us, length us, event | category | flops | bytes accessed | tf_op | source)
XLA Modules:
  0.0 502.9 jit_solution(6560523842506963549)
XLA Ops:
  9.5 11.2 %collective-permute-start = (bf16[63,512]{1,0:T(8,128)(2,1)S(1)}, bf16[63,512]{1,0:T(8,128)(2,1)S(1)}, u32[]{:S(2)}, u32[]{:S(2)}) collective-permute-start(bf16[63,512]{1,0:T(8,128)(2,1)S(1)} %slice.13), channel_id=1, source_target_pairs={{8,0},{16,8},{24,16},{32,24},{40,32},{48,40},{56,48},{64,56},{72,6... | collective-permute-start | bytes 193544 | tf_op jit(solution)/shard_map/ppermute | solution.py:14
  34.1 4.7 multiply_reduce_fusion.1
  41.9 143.9 %psum.7 = f32[]{:T(128)} all-reduce(f32[]{:T(128)S(6)} %add.41), channel_id=1, replica_groups=mesh['ctx'=64,'head'=8] {'ctx','head'}, use_global_device_ids=true, to_apply=%region_12.13 | all-reduce | flops 1 | bytes 8 | tf_op jit(solution)/shard_map/psum | solution.py:141
  191.8 12.7 %all-gather.3.cloned.1.call-done = bf16[8192,512]{1,0:T(8,128)(2,1)} async-done(((bf16[128,512]{1,0:T(8,128)(2,1)}), bf16[8192,512]{1,0:T(8,128)(2,1)}) %all-gather.3.cloned.1.call-update) | async-done | bytes 8388624 | tf_op jit(solution)/shard_map/all_gather | solution.py:58
  204.5 12.5 %reshape.91 = bf16[16,512,4,128]{3,2,1,0:T(4,128)(2,1)} reshape(bf16[8192,512]{1,0:T(8,128)(2,1)} %all-gather.3.cloned.1.call-done) | data formatting | bytes 16777216 | tf_op jit(solution)/shard_map/reshape | solution.py:63
  217.1 8.9 %copy.24 = bf16[16,512,4,128]{3,1,2,0:T(8,128)(2,1)} copy(bf16[16,512,4,128]{3,2,1,0:T(4,128)(2,1)} %reshape.91) | data formatting | bytes 16777216
  226.0 166.7 %all-gather.5.cloned.1.call-done = bf16[8192,512]{1,0:T(8,128)(2,1)} async-done(((bf16[128,512]{1,0:T(8,128)(2,1)}), bf16[8192,512]{1,0:T(8,128)(2,1)}) %all-gather.5.cloned.1.call-update) | async-done | bytes 8388624 | tf_op jit(solution)/shard_map/all_gather | solution.py:59
  392.7 12.5 %reshape.92 = bf16[16,512,4,128]{3,2,1,0:T(4,128)(2,1)} reshape(bf16[8192,512]{1,0:T(8,128)(2,1)} %all-gather.5.cloned.1.call-done) | data formatting | bytes 16777216 | tf_op jit(solution)/shard_map/reshape | solution.py:64
  405.2 8.9 %copy.26 = bf16[16,512,4,128]{3,1,2,0:T(8,128)(2,1)} copy(bf16[16,512,4,128]{3,2,1,0:T(4,128)(2,1)} %reshape.92) | data formatting | bytes 16777216
  414.1 81.2 %while.15 = (s32[]{:T(128)}, f32[4,128]{1,0:T(4,128)S(1)}, f32[4,128]{1,0:T(4,128)S(1)}, f32[4,128,128]{2,1,0:T(8,128)S(1)}, s32[16]{0:T(128)S(1)}, /*index=5*/s...) while((s32[]{:T(128)}, f32[4,128]{1,0:T(4,128)S(1)}, ...), condition=%wide.region_6.7_spmd.clone, body=%wide.region_1.6_spmd.clone.sunk | while | flops 136775296 | bytes 5152051 | solution.py:84
  416.0 3.3 conditional.3
  426.6 3.3 conditional.3
  431.9 3.3 conditional.3
  437.2 3.3 conditional.3
  442.4 3.3 conditional.3
  447.7 3.3 conditional.3
  453.0 3.3 conditional.3
  458.3 3.3 conditional.3
  463.6 3.3 conditional.3
  468.8 3.3 conditional.3
  474.1 3.3 conditional.3
  479.4 3.3 conditional.3
  484.7 3.3 conditional.3
  490.0 3.3 conditional.3
  (215 shorter events, 86.6 us)
Async XLA Ops:
  7.2 197.4 %all-gather.3.cloned.1.call-start = ((), (), s32[]{:S(2)}) async-start(), calls=%async_computation | async-start | bytes 8519680 | tf_op jit(solution)/shard_map/all_gather | solution.py:58
  7.9 384.8 %all-gather.5.cloned.1.call-start = ((), (), s32[]{:S(2)}) async-start(), calls=%async_computation.1 | async-start | bytes 8519680 | tf_op jit(solution)/shard_map/all_gather | solution.py:59
  9.5 17.6 %collective-permute-start = (bf16[63,512]{1,0:T(8,128)(2,1)S(1)}, bf16[63,512]{1,0:T(8,128)(2,1)S(1)}, u32[]{:S(2)}, u32[]{:S(2)}) collective-permute-start(bf16[63,512]{1,0:T(8,128)(2,1)S(1)} %slice.13), channel_id=1, source_target_pairs={{8,0},{16,8},{24,16},{32,24},{40,32},{48,40},{56,48},{64,56},{72,6... | collective-permute-start | bytes 193544 | tf_op jit(solution)/shard_map/ppermute | solution.py:14
  23.1 8.4 %copy-start.1 = (f32[2,4,64,256]{3,2,1,0:T(8,128)}, f32[2,4,64,256]{3,2,1,0:T(8,128)S(1)}, u32[]{:S(2)}) copy-start(f32[2,4,64,256]{3,2,1,0:T(8,128)S(1)} %fusion.34) | copy-start | bytes 1572868
  27.2 4.4 copy-start
  28.9 3.3 copy-start.2
  40.0 150.3 %collective-permute-start.1 = (bf16[63,512]{1,0:T(8,128)(2,1)}, bf16[63,512]{1,0:T(8,128)(2,1)}, u32[]{:S(2)}, u32[]{:S(2)}) collective-permute-start(bf16[63,512]{1,0:T(8,128)(2,1)} %slice.16), channel_id=1, source_target_pairs={{0,8},{8,16},{16,24},{24,32},{32,40},{40,48},{48,56},{56,64},{64,7... | collective-permute-start | bytes 193544 | tf_op jit(solution)/shard_map/ppermute | solution.py:14
Sparse Core Ops, SparseCore 0:
  12.5 192.0 all-gather.2
  209.1 183.5 all-gather.4
where the time goes:
time: 506 us; the launch traced here: 503 us
  waiting for transfers between devices  181 us (36%)
  blocking collectives  144 us (28%)
  local copies, waits for them, and re-layouts  63.2 us (12%)
  matrix products  54 us (11%)
  loops' own time  21.4 us (4%)
  between operations  16.1 us (3%)
  starting transfers between devices  13.2 us (3%)
  other arithmetic  10.2 us (2%)
    all_gather x1, waiting for transfers between devices, self_attention(): values_piece = lax.all_gather(values_local, 'ctx', axis=0, tiled=True)  167 us
    psum x1, blocking collectives, cross_attention(): overall = lax.psum(squares, ('ctx', 'head'))  144 us
    dot_general x15, matrix products, attend_block(): jnp.einsum('hrk,khd->hrd', weights.astype(jnp.bfloat16), values_block, pr...  22.8 us
    dot_general x15, matrix products, attend_block(): jnp.einsum('rhd,khd->hrk', queries, keys_block, preferred_element_type=jn...  20.6 us
    another operation x1, loops' own time, self_attention(): lax.scan(visit, folded, (key_blocks, value_blocks, jnp.arange(block_count...  20.6 us
    unnamed x12, local copies, waits for them, and re-layouts  19.6 us
    ppermute x2, starting transfers between devices, from_behind(): return lax.ppermute(block, axis, route)  13.1 us
    all_gather x1, waiting for transfers between devices, self_attention(): keys_piece = lax.all_gather(keys_local, 'ctx', axis=0, tiled=True)  12.7 us
  transfers between devices with their start and end apart: 4, of which 2 were waited for; matrix products, arithmetic and copies ran while one was open for 9% of the time, Pallas kernels for 0%

commit v1 on v0

--- a/solution.py
+++ b/solution.py
@@ -55,7 +55,12 @@
         )
     )
     folded = initial
-    keys_piece = lax.all_gather(keys_local, "ctx", axis=0, tiled=True)
+    keys_piece = jnp.concatenate(
+        jax.lax.all_to_all(
+            jnp.stack(jax.lax.psum(1, axis_name="ctx") * [keys_local], axis=0), "ctx", 0, 0
+        ),
+        axis=0,
+    )
     values_piece = lax.all_gather(values_local, "ctx", axis=0, tiled=True)
     piece_rows = keys_piece.shape[0]
     block_rows = 512

time: 506 us -> 587 us (1.16)
  the two profiles are of different devices: /device:TPU:54 before, /device:TPU:310 now
where the time goes in v1:
time: 587 us; the launch traced here: 584 us
  blocking collectives  200 us (34%)
  waiting for transfers between devices  175 us (30%)
  local copies, waits for them, and re-layouts  83 us (14%)
  matrix products  56.9 us (10%)
  loops' own time  22.2 us (4%)
  starting transfers between devices  20 us (3%)
  between operations  16.3 us (3%)
  other arithmetic  10.6 us (2%)
    psum x1, blocking collectives, cross_attention(): overall = lax.psum(squares, ('ctx', 'head'))  200 us
    ppermute x2, waiting for transfers between devices, from_behind(): return lax.ppermute(block, axis, route)  174 us
    unnamed x23, local copies, waits for them, and re-layouts  25.5 us
    dot_general x16, matrix products, attend_block(): jnp.einsum('hrk,khd->hrd', weights.astype(jnp.bfloat16), values_block, pr...  24.3 us
    dot_general x16, matrix products, attend_block(): jnp.einsum('rhd,khd->hrk', queries, keys_block, preferred_element_type=jn...  22 us
    another operation x1, loops' own time, self_attention(): lax.scan(visit, folded, (key_blocks, value_blocks, jnp.arange(block_count...  21.3 us
    all_to_all x1, starting transfers between devices, self_attention(): jax.lax.all_to_all(jnp.stack(jax.lax.psum(1, axis_name='ctx') * [keys_loc...  15.6 us
    another operation x1, local copies, waits for them, and re-layouts, self_attention(): key_blocks = keys_piece.reshape(block_count, block_rows, head_count, HD)  14 us
  transfers between devices with their start and end apart: 4, of which 1 were waited for; matrix products, arithmetic and copies ran while one was open for 10% of the time, Pallas kernels for 0%

profile of v1, /device:TPU:310, one launch (start us, length us, event | category | flops | bytes accessed | tf_op | source)
XLA Modules:
  0.0 583.9 jit_solution(6328420917868201979)
XLA Ops:
  8.2 5.2 stack.2
  13.5 15.6 %all-to-all-start = ((bf16[64,128,512]{1,2,0:T(8,128)(2,1)}), bf16[64,128,512]{1,2,0:T(8,128)(2,1)}, u32[]{:S(2)}, u32[]{:S(2)}) async-start(bf16[64,128,512]{1,2,0:T(8,128)(2,1)} %stack.2), calls=%async_computation | async-start | bytes 16777216 | tf_op jit(solution)/shard_map/all_to_all | solution.py:59
  33.9 174.2 %collective-permute-done = bf16[63,512]{1,0:T(8,128)(2,1)S(1)} collective-permute-done((bf16[63,512]{1,0:T(8,128)(2,1)S(1)}, bf16[63,512]{1,0:T(8,128)(2,1)S(1)}, u32[]{:S(2)}, u32[]{:S(2)}) %collective-permute-start) | collective-permute-done | bytes 64544 | tf_op jit(solution)/shard_map/ppermute | solution.py:14
  215.1 4.8 multiply_reduce_fusion.1
  223.1 199.9 %psum.7 = f32[]{:T(128)} all-reduce(f32[]{:T(128)S(6)} %add.41), channel_id=1, replica_groups=mesh['ctx'=64,'head'=8] {'ctx','head'}, use_global_device_ids=true, to_apply=%region_12.13 | all-reduce | flops 1 | bytes 8 | tf_op jit(solution)/shard_map/psum | solution.py:146
  429.0 12.0 %copy.42 = bf16[64,128,512]{1,0,2:T(8,128)(2,1)} copy(bf16[64,128,512]{1,2,0:T(8,128)(2,1)} %all-to-all-done) | data formatting | bytes 16777216 | tf_op jit(solution)/shard_map/all_to_all | solution.py:59
  441.0 14.0 %reshape_reshape.3 = bf16[16,512,4,128]{1,0,3,2:T(8,128)(2,1)} reshape(bf16[64,128,512]{1,0,2:T(8,128)(2,1)} %copy.42) | data formatting | bytes 16777216 | tf_op jit(solution)/shard_map/reshape;reshape | solution.py:68
  454.9 14.6 %copy.45 = bf16[16,512,4,128]{3,1,2,0:T(8,128)(2,1)} copy(bf16[16,512,4,128]{1,0,3,2:T(8,128)(2,1)} %reshape_reshape.3) | data formatting | bytes 16777216
  469.6 12.5 %reshape.89 = bf16[16,512,4,128]{3,2,1,0:T(4,128)(2,1)} reshape(bf16[8192,512]{1,0:T(8,128)(2,1)} %all-gather.2.cloned.1.call-done) | data formatting | bytes 16777216 | tf_op jit(solution)/shard_map/reshape | solution.py:69
  482.1 8.9 %copy.47 = bf16[16,512,4,128]{3,1,2,0:T(8,128)(2,1)} copy(bf16[16,512,4,128]{3,2,1,0:T(4,128)(2,1)} %reshape.89) | data formatting | bytes 16777216
  491.0 85.2 %while.15 = (s32[]{:T(128)}, f32[4,128]{1,0:T(4,128)S(1)}, f32[4,128]{1,0:T(4,128)S(1)}, f32[4,128,128]{2,1,0:T(8,128)S(1)}, s32[16]{0:T(128)S(1)}, /*index=5*/s...) while((s32[]{:T(128)}, f32[4,128]{1,0:T(4,128)S(1)}, ...), condition=%wide.region_6.7_spmd.clone, body=%wide.region_1.6_spmd.clone.sunk | while | flops 136775296 | bytes 5152051 | solution.py:89
  493.0 3.3 conditional.3
  498.3 3.3 conditional.3
  503.6 3.3 conditional.3
  509.0 3.3 conditional.3
  514.3 3.3 conditional.3
  519.6 3.3 conditional.3
  524.9 3.3 conditional.3
  530.3 3.3 conditional.3
  535.6 3.3 conditional.3
  540.9 3.3 conditional.3
  551.6 3.3 conditional.3
  562.2 3.3 conditional.3
  572.9 3.3 conditional.3
  (236 shorter events, 93.6 us)
Async XLA Ops:
  13.4 16.4 %copy-start.5 = (bf16[128,512]{1,0:T(8,128)(2,1)S(1)}, bf16[128,512]{1,0:T(8,128)(2,1)}, u32[]{:S(2)}) copy-start(bf16[128,512]{1,0:T(8,128)(2,1)} %param.14) | copy-start | bytes 393220
  13.4 18.9 %copy-start.1 = (bf16[512,512]{1,0:T(8,128)(2,1)S(1)}, bf16[512,512]{1,0:T(8,128)(2,1)}, u32[]{:S(2)}) copy-start(bf16[512,512]{1,0:T(8,128)(2,1)} %param.16) | copy-start | bytes 1572868
  13.4 19.0 %copy-start.6 = (bf16[128,512]{1,0:T(8,128)(2,1)S(1)}, bf16[128,512]{1,0:T(8,128)(2,1)}, u32[]{:S(2)}) copy-start(bf16[128,512]{1,0:T(8,128)(2,1)} %param.17) | copy-start | bytes 393220
  13.4 20.1 %copy-start.7 = (bf16[128,512]{1,0:T(8,128)(2,1)S(1)}, bf16[128,512]{1,0:T(8,128)(2,1)}, u32[]{:S(2)}) copy-start(bf16[128,512]{1,0:T(8,128)(2,1)} %param.11) | copy-start | bytes 393220
  13.5 20.3 %copy-start.2 = (bf16[512,512]{1,0:T(8,128)(2,1)S(1)}, bf16[512,512]{1,0:T(8,128)(2,1)}, u32[]{:S(2)}) copy-start(bf16[512,512]{1,0:T(8,128)(2,1)} %param.15) | copy-start | bytes 1572868
  13.5 415.5 %all-to-all-start = ((bf16[64,128,512]{1,2,0:T(8,128)(2,1)}), bf16[64,128,512]{1,2,0:T(8,128)(2,1)}, u32[]{:S(2)}, u32[]{:S(2)}) async-start(bf16[64,128,512]{1,2,0:T(8,128)(2,1)} %stack.2), calls=%async_computation | async-start | bytes 16777216 | tf_op jit(solution)/shard_map/all_to_all | solution.py:59
  29.1 440.5 %all-gather.2.cloned.1.call-start = ((), (), s32[]{:S(2)}) async-start(), calls=%async_computation.1 | async-start | bytes 8519680 | tf_op jit(solution)/shard_map/all_gather | solution.py:64
  29.8 178.3 %collective-permute-start = (bf16[63,512]{1,0:T(8,128)(2,1)S(1)}, bf16[63,512]{1,0:T(8,128)(2,1)S(1)}, u32[]{:S(2)}, u32[]{:S(2)}) collective-permute-start(bf16[63,512]{1,0:T(8,128)(2,1)S(1)} %slice.13), channel_id=1, source_target_pairs={{8,0},{16,8},{24,16},{32,24},{40,32},{48,40},{56,48},{64,56},{72,6... | collective-permute-start | bytes 193544 | tf_op jit(solution)/shard_map/ppermute | solution.py:14
  32.8 180.5 %copy-start.3 = (f32[2,4,64,256]{3,2,1,0:T(8,128)}, f32[2,4,64,256]{3,2,1,0:T(8,128)S(1)}, u32[]{:S(2)}) copy-start(f32[2,4,64,256]{3,2,1,0:T(8,128)S(1)} %fusion.34) | copy-start | bytes 1572868
  208.2 4.4 copy-start
  209.9 2.7 copy-start.4
  221.2 206.3 %collective-permute-start.1 = (bf16[63,512]{1,0:T(8,128)(2,1)}, bf16[63,512]{1,0:T(8,128)(2,1)}, u32[]{:S(2)}, u32[]{:S(2)}) collective-permute-start(bf16[63,512]{1,0:T(8,128)(2,1)} %slice.16), channel_id=1, source_target_pairs={{0,8},{8,16},{16,24},{24,32},{32,40},{40,48},{48,56},{56,64},{64,7... | collective-permute-start | bytes 193544 | tf_op jit(solution)/shard_map/ppermute | solution.py:14
Sparse Core Ops, SparseCore 0:
  34.4 381.5 all-gather.1
